TPU v7x, 512 devices: a whole 4x8x8 slice. The times are simulated.
512 devices in a mesh: pair: 64 (over z_hi, y, x), win: 8 (over z_lo, core).
Axes of the slice: x: 4, y: 8, z: 8 (z_hi: 2, z_lo: 4; z = z_hi * 4 + z_lo), core: 2. Of those that a mesh axis runs over, the one named last changes fastest.
Arguments:
- spectra: bfloat16 [32, 1024, 3, 8192], P('win', 'pair'), may hold values from -6 to 6
- pair_first: int32 [64, 64], P('pair'), may hold values from 0 to 1023, as said below
- pair_second: int32 [64, 64], P('pair'), may hold values from 0 to 1023, as said below
- pair_count: int32 [64], P('pair'), may hold values from 16 to 64, as said below
Outputs:
- stacks: float32 [4096, 9, 256], P(('pair', 'win'))
Inputs may be any that keep to these rules, and one draw needn't show every extreme that they name: Stations are numbered block by block, 16 to a block. In block b every pair_first lies in block b; pair_second lies in block b and differs from pair_first, or in block b + 1 among its first 8 stations; the last block has no pairs into a further block. Slots past pair_count hold pairs of the same kind. `pair_second`: see pair_first. `pair_count`: some block is full in every draw.
All inputs are finite; a program needn't handle non-finite values.
Results may differ from a plain program's by a relative error of at most 0.0039.
Values may be sent and summed in bfloat16 or wider, within the bound.
No kernel may reach another device: no remote copies, remote signals or barrier semaphores. Data moves between devices by JAX's collectives and lax.ppermute only.
A program may use at most 128 MiB of HBM per device.

v0:
```python
import math

import jax
import jax.numpy as jnp
from jax import lax
from jax.sharding import PartitionSpec as P

LAGS = 256


def shifted(shard, axis, by):
    peers = lax.axis_size(axis)
    pairs = [(i, i + by) for i in range(peers) if 0 <= i + by < peers]
    return lax.ppermute(shard, axis, pairs)


def lag_table(bins_count, lags_count, windows_all):
    bin_index = jnp.arange(bins_count, dtype=jnp.int32)
    lag_index = jnp.arange(lags_count, dtype=jnp.int32) - lags_count // 2
    phase_index = jnp.mod(bin_index[:, None] * lag_index[None, :], 2 * bins_count)
    angles = phase_index.astype(jnp.float32) * (jnp.pi / bins_count)
    window_taper = 0.5 + 0.5 * jnp.cos(lag_index.astype(jnp.float32) * (2.0 * jnp.pi / lags_count))
    norm_scale = 1.0 / jnp.sqrt(jnp.float32(2 * windows_all * bins_count))
    weights = (
        jnp.concatenate([jnp.cos(angles), -jnp.sin(angles)], 0)
        * (window_taper * norm_scale)[None, :]
    )
    return weights.astype(jnp.bfloat16)


def select_rows(station_table, local_ids):
    columns = jnp.arange(station_table.shape[1], dtype=jnp.int32)
    picker = (local_ids[:, None] == columns[None, :]).astype(jnp.bfloat16)
    return jnp.einsum("ps,wsck->wpck", picker, station_table, preferred_element_type=jnp.float32)


def cross_block(own_table, next_table, first_local, second_local, valid_mask, lag_weights):
    own_size = own_table.shape[1]
    left_rows = select_rows(own_table, first_local)
    right_rows = select_rows(own_table, second_local) + select_rows(
        next_table, second_local - own_size
    )
    bins_count = own_table.shape[-1] // 2
    left_real, left_imag = (left_rows[..., :bins_count], left_rows[..., bins_count:])
    right_real, right_imag = (right_rows[..., :bins_count], right_rows[..., bins_count:])
    cross_real = jnp.sum(
        left_real[:, :, :, None] * right_real[:, :, None]
        + left_imag[:, :, :, None] * right_imag[:, :, None],
        axis=0,
    )
    cross_imag = jnp.sum(
        left_imag[:, :, :, None] * right_real[:, :, None]
        - left_real[:, :, :, None] * right_imag[:, :, None],
        axis=0,
    )
    count_rows = cross_real.shape[0]
    scale_rows = valid_mask[:, None, None, None]
    real_rows = (cross_real * scale_rows).reshape(count_rows * 9, bins_count).astype(jnp.bfloat16)
    imag_rows = (cross_imag * scale_rows).reshape(count_rows * 9, bins_count).astype(jnp.bfloat16)
    result = jnp.dot(real_rows, lag_weights[:bins_count], preferred_element_type=jnp.float32)
    result = result + jnp.dot(
        imag_rows, lag_weights[bins_count:], preferred_element_type=jnp.float32
    )
    return result.reshape(count_rows, 9, lag_weights.shape[1])


def per_device(spectra, pair_first, pair_second, pair_count):
    block_size = spectra.shape[1]
    block_index = lax.axis_index("pair")
    next_stations = shifted(spectra, "pair", -1)
    windows_all = spectra.shape[0] * lax.axis_size("win")
    lag_weights = lag_table(spectra.shape[-1] // 2, LAGS, windows_all)
    block_start = block_index * block_size
    first_local = pair_first[0] - block_start
    second_local = pair_second[0] - block_start
    slot_index = jnp.arange(first_local.shape[0], dtype=jnp.int32)
    valid_mask = (slot_index < pair_count[0]).astype(jnp.float32)
    own_rows = first_local.shape[0] // lax.axis_size("win")
    block_rows = math.gcd(lax.axis_size("win") * own_rows, 16)

    def block_term(offset):
        return cross_block(
            spectra,
            next_stations,
            lax.dynamic_slice_in_dim(first_local, offset, block_rows),
            lax.dynamic_slice_in_dim(second_local, offset, block_rows),
            lax.dynamic_slice_in_dim(valid_mask, offset, block_rows),
            lag_weights,
        )

    pieces = lax.map(
        block_term, jnp.arange(0, lax.axis_size("win") * own_rows, block_rows, dtype=jnp.int32)
    )
    return lax.psum_scatter(
        pieces.reshape(lax.axis_size("win") * own_rows, 9, LAGS),
        "win",
        scatter_dimension=0,
        tiled=True,
    )


def solution(mesh):
    return jax.shard_map(
        per_device,
        mesh=mesh,
        in_specs=(P("win", "pair", None, None), P("pair", None), P("pair", None), P("pair")),
        out_specs=P(("pair", "win"), None, None),
        check_vma=False,
    )
```

profile of v0, /device:TPU:2, one launch (start us, length us, event | category | flops | bytes accessed | tf_op | source)
XLA Modules:
  0.0 394.3 jit_solution(9541903539876361651)
XLA Ops:
  6.5 7.8 %collective-permute-start = (bf16[4,16,3,8192]{3,1,2,0:T(8,128)(2,1)}, bf16[4,16,3,8192]{3,1,2,0:T(8,128)(2,1)}, u32[]{:S(2)}, u32[]{:S(2)}) collective-permute-start(bf16[4,16,3,8192]{3,1,2,0:T(8,128)(2,1)} %param.6), channel_id=1, source_target_pairs={{8,0},{16,8},{24,16},{32,24},{40,32},{48,40},{56,48},{64,56},{72,6... | collective-permute-start | bytes 9437192 | tf_op jit(solution)/shard_map/ppermute | solution.py:14
  17.4 16.5 %fusion.27 = (f32[4096,256]{1,0:T(8,128)S(1)}, f32[4096,256]{1,0:T(8,128)S(1)}) fusion(s32[256]{0:T(256)S(1)} %iota_add_fusion), kind=kLoop, calls=%fused_computation.38 | loop fusion | flops 15728640 | bytes 8389632 | tf_op jit(solution)/shard_map/cos | solution.py:25
  34.0 2.4 fusion.20
  36.4 42.2 %collective-permute-done = bf16[4,16,3,8192]{3,1,2,0:T(8,128)(2,1)} collective-permute-done((bf16[4,16,3,8192]{3,1,2,0:T(8,128)(2,1)}, bf16[4,16,3,8192]{3,1,2,0:T(8,128)(2,1)}, u32[]{:S(2)}, u32[]{:S(2)}) %collective-permute-start) | collective-permute-done | bytes 3145760 | tf_op jit(solution)/shard_map/ppermute | solution.py:14
  78.6 197.9 %while.12 = (s32[]{:T(128)}, f32[4,16,9,256]{3,1,0,2:T(8,128)}, s32[4]{0:T(128)}, s32[64]{0:T(128)}, bf16[4,16,3,8192]{3,1,2,0:T(8,128)(2,1)S(1)}, /*index=5*/s3...) while((s32[]{:T(128)}, f32[4,16,9,256]{3,1,0,2:T(8,128)}, ...), condition=%wide.region_3.4_spmd, body=%wide.region_0.3_spmd.sunk | while | flops 776639232 | bytes 127914216 | solution.py:91
  78.6 1.3 dynamic_slice.31
  83.5 5.6 %fusion.55 = f32[4,16,3,8192]{3,1,2,0:T(8,128)} fusion(f32[16,4,3,8192]{3,0,2,1:T(8,128)S(1)} %fusion.54, bf16[4,16,3,8192]{3,1,2,0:T(8,128)(2,1)} %get-tuple-element.252, s32[16]{0:T(128)S(1)} %get-tuple-element.215), kind=kOutput, calls=%fused_computation.2.clone.1 | convolution fusion | flops 51904768 | bytes 15728704 | tf_op jit(solution)/shard_map/while/body/eval_jaxpr/ps,wsck->wpck/dot_general | solution.py:34
  89.7 2.9 convolution_bitcast_fusion.2
  92.6 7.7 %fusion.56 = (f32[4,16,3,4096]{3,1,2,0:T(8,128)}, f32[4,16,3,4096]{3,1,2,0:T(8,128)}, f32[4,16,3,4096]{3,1,2,0:T(8,128)}, f32[4,16,3,4096]{3,1,2,0:T(8,128)}) fusion(f32[4,16,3,8192]{3,1,2,0:T(8,128)S(1)} %convolution_bitcast_fusion.2, f32[4,16,3,8192]{3,1,2,0:T(8,128)} %fusion.55), kind=kLoop, calls=%fused_computation.45.clone.1 | loop fusion | bytes 25165824 | tf_op jit(solution)/shard_map/while/body/eval_jaxpr/slice | solution.py:44
  100.3 7.8 %add_reduce_fusion.2 = (f32[16,3,3,4096]{3,0,2,1:T(8,128)}, f32[16,3,3,4096]{3,0,2,1:T(8,128)S(1)}) fusion(f32[4,16,3,4096]{3,1,2,0:T(8,128)} %get-tuple-element.216, f32[4,16,3,4096]{3,1,2,0:T(8,128)} %get-tuple-element.217, f32[4,16,3,4096]{3,1,2,0:T(8,128)} %get-tuple-element.218, f32[4,16,3,4096]{3,1,2,0:T(8,128)} %get-tuple-element.219), kind=kLoop, calls=%fused_computation.4.clone.1 | loop fusion | flops 17694720 | bytes 17301504 | tf_op jit(solution)/shard_map/while/body/eval_jaxpr/reduce_sum | solution.py:46
  108.1 1.6 copy.28
  109.8 2.6 reduce_sum.34
  113.4 2.8 fusion.57
  116.3 3.3 copy.29
  119.6 4.9 %reduce_sum.35 = f32[144,4096]{1,0:T(8,128)} reshape(f32[16,3,3,4096]{3,2,1,0:T(4,128)} %copy.29) | data formatting | bytes 4718592 | tf_op jit(solution)/shard_map/while/body/eval_jaxpr/reduce_sum | solution.py:46
  124.4 2.8 fusion.58
  128.0 1.3 dynamic_slice.31
  132.9 5.6 %fusion.55 = f32[4,16,3,8192]{3,1,2,0:T(8,128)} fusion(f32[16,4,3,8192]{3,0,2,1:T(8,128)S(1)} %fusion.54, bf16[4,16,3,8192]{3,1,2,0:T(8,128)(2,1)} %get-tuple-element.252, s32[16]{0:T(128)S(1)} %get-tuple-element.215), kind=kOutput, calls=%fused_computation.2.clone.1 | convolution fusion | flops 51904768 | bytes 15728704 | tf_op jit(solution)/shard_map/while/body/eval_jaxpr/ps,wsck->wpck/dot_general | solution.py:34
  139.2 2.9 convolution_bitcast_fusion.2
  142.1 7.7 %fusion.56 = (f32[4,16,3,4096]{3,1,2,0:T(8,128)}, f32[4,16,3,4096]{3,1,2,0:T(8,128)}, f32[4,16,3,4096]{3,1,2,0:T(8,128)}, f32[4,16,3,4096]{3,1,2,0:T(8,128)}) fusion(f32[4,16,3,8192]{3,1,2,0:T(8,128)S(1)} %convolution_bitcast_fusion.2, f32[4,16,3,8192]{3,1,2,0:T(8,128)} %fusion.55), kind=kLoop, calls=%fused_computation.45.clone.1 | loop fusion | bytes 25165824 | tf_op jit(solution)/shard_map/while/body/eval_jaxpr/slice | solution.py:44
  149.8 7.8 %add_reduce_fusion.2 = (f32[16,3,3,4096]{3,0,2,1:T(8,128)}, f32[16,3,3,4096]{3,0,2,1:T(8,128)S(1)}) fusion(f32[4,16,3,4096]{3,1,2,0:T(8,128)} %get-tuple-element.216, f32[4,16,3,4096]{3,1,2,0:T(8,128)} %get-tuple-element.217, f32[4,16,3,4096]{3,1,2,0:T(8,128)} %get-tuple-element.218, f32[4,16,3,4096]{3,1,2,0:T(8,128)} %get-tuple-element.219), kind=kLoop, calls=%fused_computation.4.clone.1 | loop fusion | flops 17694720 | bytes 17301504 | tf_op jit(solution)/shard_map/while/body/eval_jaxpr/reduce_sum | solution.py:46
  157.6 1.6 copy.28
  159.2 2.6 reduce_sum.34
  162.9 2.8 fusion.57
  165.7 3.3 copy.29
  169.0 4.9 %reduce_sum.35 = f32[144,4096]{1,0:T(8,128)} reshape(f32[16,3,3,4096]{3,2,1,0:T(4,128)} %copy.29) | data formatting | bytes 4718592 | tf_op jit(solution)/shard_map/while/body/eval_jaxpr/reduce_sum | solution.py:46
  173.9 2.8 fusion.58
  182.4 5.6 %fusion.55 = f32[4,16,3,8192]{3,1,2,0:T(8,128)} fusion(f32[16,4,3,8192]{3,0,2,1:T(8,128)S(1)} %fusion.54, bf16[4,16,3,8192]{3,1,2,0:T(8,128)(2,1)} %get-tuple-element.252, s32[16]{0:T(128)S(1)} %get-tuple-element.215), kind=kOutput, calls=%fused_computation.2.clone.1 | convolution fusion | flops 51904768 | bytes 15728704 | tf_op jit(solution)/shard_map/while/body/eval_jaxpr/ps,wsck->wpck/dot_general | solution.py:34
  188.6 2.9 convolution_bitcast_fusion.2
  191.5 7.7 %fusion.56 = (f32[4,16,3,4096]{3,1,2,0:T(8,128)}, f32[4,16,3,4096]{3,1,2,0:T(8,128)}, f32[4,16,3,4096]{3,1,2,0:T(8,128)}, f32[4,16,3,4096]{3,1,2,0:T(8,128)}) fusion(f32[4,16,3,8192]{3,1,2,0:T(8,128)S(1)} %convolution_bitcast_fusion.2, f32[4,16,3,8192]{3,1,2,0:T(8,128)} %fusion.55), kind=kLoop, calls=%fused_computation.45.clone.1 | loop fusion | bytes 25165824 | tf_op jit(solution)/shard_map/while/body/eval_jaxpr/slice | solution.py:44
  199.2 7.8 %add_reduce_fusion.2 = (f32[16,3,3,4096]{3,0,2,1:T(8,128)}, f32[16,3,3,4096]{3,0,2,1:T(8,128)S(1)}) fusion(f32[4,16,3,4096]{3,1,2,0:T(8,128)} %get-tuple-element.216, f32[4,16,3,4096]{3,1,2,0:T(8,128)} %get-tuple-element.217, f32[4,16,3,4096]{3,1,2,0:T(8,128)} %get-tuple-element.218, f32[4,16,3,4096]{3,1,2,0:T(8,128)} %get-tuple-element.219), kind=kLoop, calls=%fused_computation.4.clone.1 | loop fusion | flops 17694720 | bytes 17301504 | tf_op jit(solution)/shard_map/while/body/eval_jaxpr/reduce_sum | solution.py:46
  207.0 1.6 copy.28
  208.7 2.6 reduce_sum.34
  212.4 2.8 fusion.57
  215.2 3.3 copy.29
  218.5 4.9 %reduce_sum.35 = f32[144,4096]{1,0:T(8,128)} reshape(f32[16,3,3,4096]{3,2,1,0:T(4,128)} %copy.29) | data formatting | bytes 4718592 | tf_op jit(solution)/shard_map/while/body/eval_jaxpr/reduce_sum | solution.py:46
  223.3 2.8 fusion.58
  231.8 5.6 %fusion.55 = f32[4,16,3,8192]{3,1,2,0:T(8,128)} fusion(f32[16,4,3,8192]{3,0,2,1:T(8,128)S(1)} %fusion.54, bf16[4,16,3,8192]{3,1,2,0:T(8,128)(2,1)} %get-tuple-element.252, s32[16]{0:T(128)S(1)} %get-tuple-element.215), kind=kOutput, calls=%fused_computation.2.clone.1 | convolution fusion | flops 51904768 | bytes 15728704 | tf_op jit(solution)/shard_map/while/body/eval_jaxpr/ps,wsck->wpck/dot_general | solution.py:34
  238.1 2.9 convolution_bitcast_fusion.2
  241.0 7.7 %fusion.56 = (f32[4,16,3,4096]{3,1,2,0:T(8,128)}, f32[4,16,3,4096]{3,1,2,0:T(8,128)}, f32[4,16,3,4096]{3,1,2,0:T(8,128)}, f32[4,16,3,4096]{3,1,2,0:T(8,128)}) fusion(f32[4,16,3,8192]{3,1,2,0:T(8,128)S(1)} %convolution_bitcast_fusion.2, f32[4,16,3,8192]{3,1,2,0:T(8,128)} %fusion.55), kind=kLoop, calls=%fused_computation.45.clone.1 | loop fusion | bytes 25165824 | tf_op jit(solution)/shard_map/while/body/eval_jaxpr/slice | solution.py:44
  248.7 7.8 %add_reduce_fusion.2 = (f32[16,3,3,4096]{3,0,2,1:T(8,128)}, f32[16,3,3,4096]{3,0,2,1:T(8,128)S(1)}) fusion(f32[4,16,3,4096]{3,1,2,0:T(8,128)} %get-tuple-element.216, f32[4,16,3,4096]{3,1,2,0:T(8,128)} %get-tuple-element.217, f32[4,16,3,4096]{3,1,2,0:T(8,128)} %get-tuple-element.218, f32[4,16,3,4096]{3,1,2,0:T(8,128)} %get-tuple-element.219), kind=kLoop, calls=%fused_computation.4.clone.1 | loop fusion | flops 17694720 | bytes 17301504 | tf_op jit(solution)/shard_map/while/body/eval_jaxpr/reduce_sum | solution.py:46
  256.5 1.6 copy.28
  258.1 2.6 reduce_sum.34
  261.8 2.8 fusion.57
  264.7 3.3 copy.29
  267.9 4.9 %reduce_sum.35 = f32[144,4096]{1,0:T(8,128)} reshape(f32[16,3,3,4096]{3,2,1,0:T(4,128)} %copy.29) | data formatting | bytes 4718592 | tf_op jit(solution)/shard_map/while/body/eval_jaxpr/reduce_sum | solution.py:46
  272.8 2.8 fusion.58
  276.5 111.0 %reduce-scatter.2.cloned.1.call-done = f32[8,9,256]{2,0,1:T(8,128)} async-done(((f32[64,9,256]{2,0,1:T(8,128)}), f32[8,9,256]{2,0,1:T(8,128)}) %reduce-scatter.2.cloned.1.call-update) | async-done | bytes 73744 | tf_op jit(solution)/shard_map/reduce_scatter | solution.py:94
  (60 shorter events, 22.3 us)
Async XLA Ops:
  6.5 380.9 %reduce-scatter.2.cloned.1.call-start = ((), (), s32[]{:S(2)}) async-start(), calls=%async_computation.1 | async-start | bytes 663552 | tf_op jit(solution)/shard_map/reduce_scatter | solution.py:94
  6.5 72.0 %collective-permute-start = (bf16[4,16,3,8192]{3,1,2,0:T(8,128)(2,1)}, bf16[4,16,3,8192]{3,1,2,0:T(8,128)(2,1)}, u32[]{:S(2)}, u32[]{:S(2)}) collective-permute-start(bf16[4,16,3,8192]{3,1,2,0:T(8,128)(2,1)} %param.6), channel_id=1, source_target_pairs={{8,0},{16,8},{24,16},{32,24},{40,32},{48,40},{56,48},{64,56},{72,6... | collective-permute-start | bytes 9437192 | tf_op jit(solution)/shard_map/ppermute | solution.py:14
  34.0 44.6 %copy-start = (bf16[4,16,3,8192]{3,1,2,0:T(8,128)(2,1)S(1)}, bf16[4,16,3,8192]{3,1,2,0:T(8,128)(2,1)}, u32[]{:S(2)}) copy-start(bf16[4,16,3,8192]{3,1,2,0:T(8,128)(2,1)} %param.6) | copy-start | bytes 9437188
  112.3 3.9 copy-start.2
  119.5 8.5 %copy-start.1 = (bf16[4,16,3,8192]{3,1,2,0:T(8,128)(2,1)S(1)}, bf16[4,16,3,8192]{3,1,2,0:T(8,128)(2,1)}, u32[]{:S(2)}) copy-start(bf16[4,16,3,8192]{3,1,2,0:T(8,128)(2,1)} %get-tuple-element.272) | copy-start | bytes 9437188 | tf_op jit(solution)/shard_map/while
  161.8 3.9 %copy-start.2 = (f32[16,3,3,4096]{3,0,2,1:T(8,128)S(1)}, f32[16,3,3,4096]{3,0,2,1:T(8,128)}, u32[]{:S(2)}) copy-start(f32[16,3,3,4096]{3,0,2,1:T(8,128)} %get-tuple-element.221) | copy-start | bytes 7077892 | tf_op jit(solution)/shard_map/while
  169.0 8.5 %copy-start.1 = (bf16[4,16,3,8192]{3,1,2,0:T(8,128)(2,1)S(1)}, bf16[4,16,3,8192]{3,1,2,0:T(8,128)(2,1)}, u32[]{:S(2)}) copy-start(bf16[4,16,3,8192]{3,1,2,0:T(8,128)(2,1)} %get-tuple-element.272) | copy-start | bytes 9437188 | tf_op jit(solution)/shard_map/while
  211.3 3.9 %copy-start.2 = (f32[16,3,3,4096]{3,0,2,1:T(8,128)S(1)}, f32[16,3,3,4096]{3,0,2,1:T(8,128)}, u32[]{:S(2)}) copy-start(f32[16,3,3,4096]{3,0,2,1:T(8,128)} %get-tuple-element.221) | copy-start | bytes 7077892 | tf_op jit(solution)/shard_map/while
  218.5 8.5 %copy-start.1 = (bf16[4,16,3,8192]{3,1,2,0:T(8,128)(2,1)S(1)}, bf16[4,16,3,8192]{3,1,2,0:T(8,128)(2,1)}, u32[]{:S(2)}) copy-start(bf16[4,16,3,8192]{3,1,2,0:T(8,128)(2,1)} %get-tuple-element.272) | copy-start | bytes 9437188 | tf_op jit(solution)/shard_map/while
  260.7 3.9 %copy-start.2 = (f32[16,3,3,4096]{3,0,2,1:T(8,128)S(1)}, f32[16,3,3,4096]{3,0,2,1:T(8,128)}, u32[]{:S(2)}) copy-start(f32[16,3,3,4096]{3,0,2,1:T(8,128)} %get-tuple-element.221) | copy-start | bytes 7077892 | tf_op jit(solution)/shard_map/while
  267.9 8.5 %copy-start.1 = (bf16[4,16,3,8192]{3,1,2,0:T(8,128)(2,1)S(1)}, bf16[4,16,3,8192]{3,1,2,0:T(8,128)(2,1)}, u32[]{:S(2)}) copy-start(bf16[4,16,3,8192]{3,1,2,0:T(8,128)(2,1)} %get-tuple-element.272) | copy-start | bytes 9437188 | tf_op jit(solution)/shard_map/while
Sparse Core Ops, SparseCore 0:
  276.6 110.8 reduce-scatter.1
where the time goes:
time: 395 us; the launch traced here: 394 us
  waiting for transfers between devices  153 us (39%)
  local copies, waits for them, and re-layouts  95.5 us (24%)
  matrix products  60.6 us (15%)
  other arithmetic  55.5 us (14%)
  between operations  14.1 us (4%)
  starting transfers between devices  7.78 us (2%)
  loops' own time  7.67 us (2%)
    reduce_scatter x1, waiting for transfers between devices, per_device(): lax.psum_scatter(pieces.reshape(lax.axis_size('win') * own_rows, 9, LAGS)...  111 us
    ppermute x1, waiting for transfers between devices, shifted(): return lax.ppermute(shard, axis, pairs)  42.2 us
    dot_general x12, matrix products, select_rows(): jnp.einsum('ps,wsck->wpck', picker, station_table, preferred_element_type...  38 us
    reduce_sum x8, local copies, waits for them, and re-layouts, cross_block(): jnp.sum(left_real[:, :, :, None] * right_real[:, :, None] + left_imag[:,...  32.5 us
    reduce_sum x4, other arithmetic, cross_block(): jnp.sum(left_real[:, :, :, None] * right_real[:, :, None] + left_imag[:,...  31.3 us
    slice x4, local copies, waits for them, and re-layouts, cross_block(): left_rows[..., :bins_count]  30.8 us
    reduce_sum x8, local copies, waits for them, and re-layouts, cross_block(): jnp.sum(left_imag[:, :, :, None] * right_real[:, :, None] - left_real[:,...  16.8 us
    cos x1, other arithmetic, lag_table(): jnp.cos(angles)  16.5 us
  transfers between devices with their start and end apart: 2, of which 2 were waited for; matrix products, arithmetic and copies ran while one was open for 5% of the time, Pallas kernels for 0%

commit v1 on v0

v1 whole, which is shorter than its diff:
```python
import jax
import jax.numpy as jnp
from jax import lax
from jax.experimental import pallas as pl
from jax.experimental.pallas import tpu as pltpu
from jax.sharding import PartitionSpec as P

LAGS = 256
CHUNK = 512


def shifted(shard, axis, by):
    peers = lax.axis_size(axis)
    pairs = [(i, i + by) for i in range(peers) if 0 <= i + by < peers]
    return lax.ppermute(shard, axis, pairs)


def lag_table(bins_count, lags_count, windows_all):
    bin_index = jnp.arange(bins_count, dtype=jnp.int32)
    lag_index = jnp.arange(lags_count, dtype=jnp.int32) - lags_count // 2
    phase_index = jnp.mod(bin_index[:, None] * lag_index[None, :], 2 * bins_count)
    angles = phase_index.astype(jnp.float32) * (jnp.pi / bins_count)
    window_taper = 0.5 + 0.5 * jnp.cos(lag_index.astype(jnp.float32) * (2.0 * jnp.pi / lags_count))
    norm_scale = 1.0 / jnp.sqrt(jnp.float32(2 * windows_all * bins_count))
    weights = (
        jnp.concatenate([jnp.cos(angles), -jnp.sin(angles)], 0)
        * (window_taper * norm_scale)[None, :]
    )
    return weights.astype(jnp.bfloat16)


def stack_kernel(n_win, n_comp, owners, lr_ref, li_ref, rr_ref, ri_ref, valid_ref, wr_ref, wi_ref, out_ref):
    @pl.when(pl.program_id(0) == 0)
    def _():
        out_ref[...] = jnp.zeros_like(out_ref)

    valid = valid_ref[...]
    wr = wr_ref[...]
    wi = wi_ref[...]
    slots = lr_ref.shape[1]
    for a in range(n_comp):
        lr = [lr_ref[w * n_comp + a].astype(jnp.float32) for w in range(n_win)]
        li = [li_ref[w * n_comp + a].astype(jnp.float32) for w in range(n_win)]
        for c in range(n_comp):
            re = None
            im = None
            for w in range(n_win):
                rr = rr_ref[w * n_comp + c].astype(jnp.float32)
                ri = ri_ref[w * n_comp + c].astype(jnp.float32)
                re_w = lr[w] * rr + li[w] * ri
                im_w = li[w] * rr - lr[w] * ri
                re = re_w if re is None else re + re_w
                im = im_w if im is None else im + im_w
            re = (re * valid).astype(jnp.bfloat16)
            im = (im * valid).astype(jnp.bfloat16)
            term = jnp.dot(re, wr, preferred_element_type=jnp.float32)
            term = term + jnp.dot(im, wi, preferred_element_type=jnp.float32)
            ac = a * n_comp + c
            out_ref[:, ac] += term.reshape(owners, slots // owners, term.shape[-1])


def stacks_of(left, right, valid, lag_weights, owners):
    rows, slots, twice = left.shape
    bins_count = twice // 2
    n_comp = 3
    n_win = rows // n_comp
    steps = bins_count // CHUNK
    lags = lag_weights.shape[1]
    spec_re = pl.BlockSpec((rows, slots, CHUNK), lambda k: (0, 0, k))
    spec_im = pl.BlockSpec((rows, slots, CHUNK), lambda k: (0, 0, k + steps))
    kernel = lambda *refs: stack_kernel(n_win, n_comp, owners, *refs)
    flops = 2 * slots * 9 * twice * lags + 8 * slots * 9 * bins_count * n_win
    bytes_accessed = 2 * left.size * 2 + lag_weights.size * 2 + owners * 9 * slots * lags * 4
    return pl.pallas_call(
        kernel,
        grid=(steps,),
        in_specs=[
            spec_re,
            spec_im,
            spec_re,
            spec_im,
            pl.BlockSpec((slots, 1), lambda k: (0, 0)),
            pl.BlockSpec((CHUNK, lags), lambda k: (k, 0)),
            pl.BlockSpec((CHUNK, lags), lambda k: (k + steps, 0)),
        ],
        out_specs=pl.BlockSpec((owners, 9, slots // owners, lags), lambda k: (0, 0, 0, 0)),
        out_shape=jax.ShapeDtypeStruct((owners, 9, slots // owners, lags), jnp.float32),
        compiler_params=pltpu.CompilerParams(
            dimension_semantics=("arbitrary",), vmem_limit_bytes=48 * 1024 * 1024
        ),
        cost_estimate=pl.CostEstimate(
            flops=flops, transcendentals=0, bytes_accessed=bytes_accessed
        ),
    )(left, left, right, right, valid, lag_weights, lag_weights)


def per_device(spectra, pair_first, pair_second, pair_count):
    block_size = spectra.shape[1]
    owners = lax.axis_size("win")
    block_index = lax.axis_index("pair")
    next_stations = shifted(spectra[:, : block_size // 2], "pair", -1)
    windows_all = spectra.shape[0] * owners
    lag_weights = lag_table(spectra.shape[-1] // 2, LAGS, windows_all)
    block_start = block_index * block_size
    first_local = pair_first[0] - block_start
    second_local = pair_second[0] - block_start
    slots = first_local.shape[0]
    slot_index = jnp.arange(slots, dtype=jnp.int32)
    valid = (slot_index < pair_count[0]).astype(jnp.float32)[:, None]

    table = jnp.concatenate([spectra, next_stations], axis=1)
    left = jnp.take(spectra, first_local, axis=1, mode="clip")
    right = jnp.take(table, second_local, axis=1, mode="clip")
    n_w, _, n_c, twice = spectra.shape
    left = jnp.transpose(left, (0, 2, 1, 3)).reshape(n_w * n_c, slots, twice)
    right = jnp.transpose(right, (0, 2, 1, 3)).reshape(n_w * n_c, slots, twice)

    partial = stacks_of(left, right, valid, lag_weights, owners)
    received = lax.all_to_all(partial, "win", 0, 0, tiled=True)
    mine = jnp.sum(received, axis=0)
    return jnp.transpose(mine, (1, 0, 2))


def solution(mesh):
    return jax.shard_map(
        per_device,
        mesh=mesh,
        in_specs=(P("win", "pair", None, None), P("pair", None), P("pair", None), P("pair")),
        out_specs=P(("pair", "win"), None, None),
        check_vma=False,
    )
```

time: 395 us -> 166 us (0.42)
  the two profiles are of different devices: /device:TPU:2 before, /device:TPU:62 now
where the time goes in v1:
time: 166 us; the launch traced here: 165 us
  local copies, waits for them, and re-layouts  78.3 us (47%)
  other arithmetic  30.5 us (18%)
  blocking collectives  24.2 us (15%)
  Pallas kernels  19.3 us (12%)
  waiting for transfers between devices  9.41 us (6%)
  starting transfers between devices  2.73 us (2%)
    gather x1, local copies, waits for them, and re-layouts, per_device(): left = jnp.take(spectra, first_local, axis=1, mode='clip')  40 us
    all_to_all x1, blocking collectives, per_device(): received = lax.all_to_all(partial, 'win', 0, 0, tiled=True)  24.2 us
    pallas_call x1, Pallas kernels, stacks_of(): pl.pallas_call(kernel, grid=(steps,), in_specs=[spec_re, spec_im, spec_re...  19.3 us
    cos x1, other arithmetic, lag_table(): jnp.cos(angles)  18 us
    gather x1, local copies, waits for them, and re-layouts, per_device(): right = jnp.take(table, second_local, axis=1, mode='clip')  15.8 us
    transpose x1, local copies, waits for them, and re-layouts, per_device(): right = jnp.transpose(right, (0, 2, 1, 3)).reshape(n_w * n_c, slots, twice)  14.7 us
    ppermute x1, waiting for transfers between devices, shifted(): return lax.ppermute(shard, axis, pairs)  9.41 us
    concatenate x1, other arithmetic, per_device(): table = jnp.concatenate([spectra, next_stations], axis=1)  6.53 us
  transfers between devices with their start and end apart: 1, of which 1 were waited for; matrix products, arithmetic and copies ran while one was open for 38% of the time, Pallas kernels for 0%

profile of v1, /device:TPU:62, one launch (start us, length us, event | category | flops | bytes accessed | tf_op | source)
XLA Modules:
  0.0 165.2 jit_solution(7829297472245463831)
XLA Ops:
  0.0 0.0 copy-start.4
  0.0 0.0 copy-start.5
  0.0 4.3 %copy.6 = bf16[4,16,3,8192]{3,0,2,1:T(4,128)(2,1)S(1)} copy(bf16[4,16,3,8192]{3,1,2,0:T(8,128)(2,1)} %param.4) | data formatting | bytes 6291456 | tf_op args[0]
  4.4 0.0 copy-start.2
  4.4 1.7 %copy-done.2 = bf16[4,16,3,8192]{3,0,2,1:T(4,128)(2,1)} copy-done((bf16[4,16,3,8192]{3,0,2,1:T(4,128)(2,1)}, bf16[4,16,3,8192]{3,0,2,1:T(4,128)(2,1)S(1)}, u32[]{:S(2)}) %copy-start.2) | copy-done | bytes 3145752
  6.0 1.9 %slice.8 = bf16[4,8,3,8192]{3,0,2,1:T(4,128)(2,1)} slice(bf16[4,16,3,8192]{3,0,2,1:T(4,128)(2,1)S(1)} %copy.6), slice={[0:4], [0:8], [0:3], [0:8192]} | slice | bytes 3145728 | tf_op jit(solution)/shard_map/slice | solution.py:101
  7.9 2.7 %collective-permute-start = (bf16[4,8,3,8192]{3,0,2,1:T(4,128)(2,1)}, bf16[4,8,3,8192]{3,0,2,1:T(4,128)(2,1)}, u32[]{:S(2)}, u32[]{:S(2)}) collective-permute-start(bf16[4,8,3,8192]{3,0,2,1:T(4,128)(2,1)} %slice.8), channel_id=1, source_target_pairs={{8,0},{16,8},{24,16},{32,24},{40,32},{48,40},{56,48},{64,56},{72,6... | collective-permute-start | bytes 4718600 | tf_op jit(solution)/shard_map/ppermute | solution.py:15
  11.3 0.0 copy-done.4
  11.4 0.0 copy-done.5
  11.4 0.0 copy-start.1
  11.4 18.0 %fusion.7 = (f32[4096,256]{1,0:T(8,128)}, f32[4096,256]{1,0:T(8,128)}) fusion(s32[256]{0:T(256)S(1)} %iota_add_fusion), kind=kLoop, calls=%fused_computation.15 | loop fusion | flops 15728640 | bytes 8389632 | tf_op jit(solution)/shard_map/cos | solution.py:26
  29.5 0.0 copy-done.1
  29.5 40.0 %gather_fusion = bf16[64,4,3,8192]{3,0,2,1:T(8,128)(2,1)} fusion(bf16[4,16,3,8192]{3,1,2,0:T(8,128)(2,1)S(1)} %copy-done.1, s32[1024]{0:T(1024)S(1)} %pad_clamp_fusion.1), kind=kCustom, calls=%fused_computation | custom fusion | bytes 25166080 | tf_op jit(solution)/shard_map/jit(_take)/gather | solution.py:112
  69.4 0.0 copy-start.3
  69.4 5.2 %fusion.refs_5_.refs_6_ = bf16[8192,256]{1,0:T(8,128)(2,1)} fusion(f32[4096,256]{1,0:T(8,128)} %get-tuple-element.6, f32[4096,256]{1,0:T(8,128)} %get-tuple-element.5, f32[256]{0:T(256)S(1)} %add_multiply_fusion), kind=kLoop, calls=%fused_computation.3 | loop fusion | flops 6291456 | bytes 12583936 | tf_op jit(solution)/shard_map/convert_element_type | solution.py:29
  74.6 9.4 %collective-permute-done = bf16[4,8,3,8192]{3,0,2,1:T(4,128)(2,1)} collective-permute-done((bf16[4,8,3,8192]{3,0,2,1:T(4,128)(2,1)}, bf16[4,8,3,8192]{3,0,2,1:T(4,128)(2,1)}, u32[]{:S(2)}, u32[]{:S(2)}) %collective-permute-start) | collective-permute-done | bytes 1572896 | tf_op jit(solution)/shard_map/ppermute | solution.py:15
  84.0 0.0 copy-done.3
  84.0 6.5 %pad_maximum_fusion = bf16[4,24,3,8192]{3,0,2,1:T(4,128)(2,1)} fusion(bf16[4,8,3,8192]{3,0,2,1:T(4,128)(2,1)} %collective-permute-done, bf16[4,16,3,8192]{3,0,2,1:T(4,128)(2,1)S(1)} %copy-done.3), kind=kLoop, calls=%fused_computation.7 | loop fusion | flops 2359296 | bytes 9437184 | tf_op jit(solution)/shard_map/concatenate | solution.py:111
  90.6 15.8 %gather_fusion.1 = bf16[64,4,3,8192]{3,1,2,0:T(4,128)(2,1)} fusion(bf16[4,24,3,8192]{3,0,2,1:T(4,128)(2,1)} %pad_maximum_fusion, s32[1024]{0:T(1024)S(1)} %pad_clamp_fusion), kind=kCustom, calls=%fused_computation.1 | custom fusion | bytes 25166080 | tf_op jit(solution)/shard_map/jit(_take)/gather | solution.py:113
  106.3 0.0 copy-start
  106.3 14.7 %copy.7 = bf16[4,3,64,8192]{3,2,1,0:T(8,128)(2,1)} copy(bf16[4,3,64,8192]{3,0,1,2:T(4,128)(2,1)} %bitcast.16) | data formatting | bytes 25165824 | tf_op jit(solution)/shard_map/transpose | solution.py:116
  121.0 0.0 copy-done
  121.0 19.3 %shard_map.46 = f32[8,9,8,256]{3,2,1,0:T(8,128)S(1)} custom-call(bf16[12,64,8192]{2,1,0:T(8,128)(2,1)} %bitcast.12, bf16[12,64,8192]{2,1,0:T(8,128)(2,1)} %bitcast.13, bf16[12,64,8192]{2,1,0:T(8,128)(2,1)} %bitcast.14, bf16[12,64,8192]{2,1,0:T(8,128)(2,1)} %bitcast.15, f32[64,1]{1,0:T(8,128)S(1)} %fusion.8.refs_4_, bf16[8192,256]{1,0:T(8,128)(2,1)S(1)} %copy-done, ...), custom_call_target="tpu_custom_call" | custom-call | flops 2491416576 | bytes 34078720 | tf_op jit(solution)/shard_map/pallas_call | solution.py:74
  140.3 24.2 %all_to_all.5 = f32[8,9,8,256]{3,2,1,0:T(8,128)S(1)} all-to-all(f32[8,9,8,256]{3,2,1,0:T(8,128)S(1)} %shard_map.46), channel_id=1, replica_groups=mesh['pair'=64,'win'=8] {'win'}, dimensions={0} | all-to-all | bytes 1179648 | tf_op jit(solution)/shard_map/all_to_all | solution.py:119
  164.5 0.7 reduce_sum.9
  (7 shorter events, 0.1 us)
Async XLA Ops:
  0.0 11.4 %copy-start.4 = (s32[1,64]{1,0:T(1,128)S(1)}, s32[1,64]{1,0:T(1,128)}, u32[]{:S(2)}) copy-start(s32[1,64]{1,0:T(1,128)} %param.5) | copy-start | bytes 772
  0.0 11.4 %copy-start.5 = (s32[1,64]{1,0:T(1,128)S(1)}, s32[1,64]{1,0:T(1,128)}, u32[]{:S(2)}) copy-start(s32[1,64]{1,0:T(1,128)} %param.6) | copy-start | bytes 772
  4.4 1.7 %copy-start.2 = (bf16[4,16,3,8192]{3,0,2,1:T(4,128)(2,1)}, bf16[4,16,3,8192]{3,0,2,1:T(4,128)(2,1)S(1)}, u32[]{:S(2)}) copy-start(bf16[4,16,3,8192]{3,0,2,1:T(4,128)(2,1)S(1)} %copy.6) | copy-start | bytes 9437188
  7.9 76.1 %collective-permute-start = (bf16[4,8,3,8192]{3,0,2,1:T(4,128)(2,1)}, bf16[4,8,3,8192]{3,0,2,1:T(4,128)(2,1)}, u32[]{:S(2)}, u32[]{:S(2)}) collective-permute-start(bf16[4,8,3,8192]{3,0,2,1:T(4,128)(2,1)} %slice.8), channel_id=1, source_target_pairs={{8,0},{16,8},{24,16},{32,24},{40,32},{48,40},{56,48},{64,56},{72,6... | collective-permute-start | bytes 4718600 | tf_op jit(solution)/shard_map/ppermute | solution.py:15
  11.4 18.0 %copy-start.1 = (bf16[4,16,3,8192]{3,1,2,0:T(8,128)(2,1)S(1)}, bf16[4,16,3,8192]{3,1,2,0:T(8,128)(2,1)}, u32[]{:S(2)}) copy-start(bf16[4,16,3,8192]{3,1,2,0:T(8,128)(2,1)} %param.4) | copy-start | bytes 9437188
  69.4 14.6 %copy-start.3 = (bf16[4,16,3,8192]{3,0,2,1:T(4,128)(2,1)S(1)}, bf16[4,16,3,8192]{3,0,2,1:T(4,128)(2,1)}, u32[]{:S(2)}) copy-start(bf16[4,16,3,8192]{3,0,2,1:T(4,128)(2,1)} %copy-done.2) | copy-start | bytes 9437188
  106.3 14.7 %copy-start = (bf16[8192,256]{1,0:T(8,128)(2,1)S(1)}, bf16[8192,256]{1,0:T(8,128)(2,1)}, u32[]{:S(2)}) copy-start(bf16[8192,256]{1,0:T(8,128)(2,1)} %fusion.refs_5_.refs_6_) | copy-start | bytes 12582916

commit v2 on v1

--- a/solution.py
+++ b/solution.py
@@ -108,12 +108,16 @@
     slot_index = jnp.arange(slots, dtype=jnp.int32)
     valid = (slot_index < pair_count[0]).astype(jnp.float32)[:, None]
 
-    table = jnp.concatenate([spectra, next_stations], axis=1)
-    left = jnp.take(spectra, first_local, axis=1, mode="clip")
-    right = jnp.take(table, second_local, axis=1, mode="clip")
     n_w, _, n_c, twice = spectra.shape
-    left = jnp.transpose(left, (0, 2, 1, 3)).reshape(n_w * n_c, slots, twice)
-    right = jnp.transpose(right, (0, 2, 1, 3)).reshape(n_w * n_c, slots, twice)
+    own_rows = jnp.transpose(spectra, (0, 2, 1, 3)).reshape(n_w * n_c, block_size, twice)
+    next_rows = jnp.transpose(next_stations, (0, 2, 1, 3)).reshape(n_w * n_c, block_size // 2, twice)
+    table = jnp.concatenate([own_rows, next_rows], axis=1)
+    own_cols = jnp.arange(block_size, dtype=jnp.int32)
+    table_cols = jnp.arange(table.shape[1], dtype=jnp.int32)
+    pick_first = (first_local[:, None] == own_cols[None, :]).astype(jnp.bfloat16)
+    pick_second = (second_local[:, None] == table_cols[None, :]).astype(jnp.bfloat16)
+    left = jnp.einsum("ps,xsk->xpk", pick_first, own_rows, preferred_element_type=jnp.bfloat16)
+    right = jnp.einsum("ps,xsk->xpk", pick_second, table, preferred_element_type=jnp.bfloat16)
 
     partial = stacks_of(left, right, valid, lag_weights, owners)
     received = lax.all_to_all(partial, "win", 0, 0, tiled=True)

time: 166 us -> 134 us (0.81)
  local copies, waits for them, and re-layouts: 78.3 us -> 2.72 us
  waiting for transfers between devices: 9.41 us -> 45.6 us
  matrix products: 0 us -> 16 us
  other arithmetic: 30.5 us -> 21.3 us
    gather x2 -> x0, local copies, waits for them, and re-layouts: 55.7 us -> none  [the longest x1 40 us: per_device(): left = jnp.take(spectra, first_local, axis=1, mode='clip')]
    ppermute x1, waiting for transfers between devices: 9.41 us -> 45.6 us  [shifted(): return lax.ppermute(shard, axis, pairs)]
    dot_general x0 -> x2, matrix products: none -> 16 us  [the longest x1 9.59 us: per_device(): jnp.einsum('ps,xsk->xpk', pick_second, table, preferred_element_type=jnp....]
    transpose x1 -> x0, local copies, waits for them, and re-layouts: 14.7 us -> none  [per_device(): right = jnp.transpose(right, (0, 2, 1, 3)).reshape(n_w * n_c, slots, twice)]
    concatenate x1 -> x0, other arithmetic: 6.53 us -> none  [per_device(): table = jnp.concatenate([spectra, next_stations], axis=1)]
    unnamed x13 -> x8, local copies, waits for them, and re-layouts: 6.04 us -> 0.02 us
    convert_element_type x1, other arithmetic: 5.19 us -> 2.58 us  [lag_table(): return weights.astype(jnp.bfloat16)]
  transfers between devices with their start and end apart: 1 -> 1, of which waited for: 1 -> 1; matrix products, arithmetic and copies ran while one was open for 38% -> 20% of each run, Pallas kernels for 0% -> 0%
where the time goes in v2:
time: 134 us
  waiting for transfers between devices  45.6 us (34%)
  blocking collectives  24.4 us (18%)
  other arithmetic  21.3 us (16%)
  Pallas kernels  20.2 us (15%)
  matrix products  16 us (12%)
  starting transfers between devices  2.73 us (2%)
  local copies, waits for them, and re-layouts  2.72 us (2%)
    ppermute x1, waiting for transfers between devices, shifted(): return lax.ppermute(shard, axis, pairs)  45.6 us
    all_to_all x1, blocking collectives, per_device(): received = lax.all_to_all(partial, 'win', 0, 0, tiled=True)  24.4 us
    pallas_call x1, Pallas kernels, stacks_of(): pl.pallas_call(kernel, grid=(steps,), in_specs=[spec_re, spec_im, spec_re...  20.2 us
    cos x1, other arithmetic, lag_table(): jnp.cos(angles)  18 us
    dot_general x1, matrix products, per_device(): jnp.einsum('ps,xsk->xpk', pick_second, table, preferred_element_type=jnp....  9.59 us
    dot_general x1, matrix products, per_device(): jnp.einsum('ps,xsk->xpk', pick_first, own_rows, preferred_element_type=jn...  6.4 us
    ppermute x1, starting transfers between devices, shifted(): return lax.ppermute(shard, axis, pairs)  2.73 us
    slice x1, local copies, waits for them, and re-layouts, per_device(): next_stations = shifted(spectra[:, :block_size // 2], 'pair', -1)  2.7 us
  transfers between devices with their start and end apart: 1, of which 1 were waited for; matrix products, arithmetic and copies ran while one was open for 20% of the time, Pallas kernels for 0%

profile of v2, /device:TPU:62, one launch (start us, length us, event | category | flops | bytes accessed | tf_op | source)
XLA Modules:
  0.0 133.7 jit_solution(4087508059836980656)
XLA Ops:
  0.0 2.7 %slice.3 = bf16[4,8,3,8192]{3,1,2,0:T(8,128)(2,1)} slice(bf16[4,16,3,8192]{3,1,2,0:T(8,128)(2,1)} %param.4), slice={[0:4], [0:8], [0:3], [0:8192]} | slice | bytes 3145728 | tf_op jit(solution)/shard_map/slice | solution.py:101
  2.7 2.7 %collective-permute-start = (bf16[4,8,3,8192]{3,1,2,0:T(8,128)(2,1)}, bf16[4,8,3,8192]{3,1,2,0:T(8,128)(2,1)}, u32[]{:S(2)}, u32[]{:S(2)}) collective-permute-start(bf16[4,8,3,8192]{3,1,2,0:T(8,128)(2,1)} %slice.3), channel_id=1, source_target_pairs={{8,0},{16,8},{24,16},{32,24},{40,32},{48,40},{56,48},{64,56},{72,6... | collective-permute-start | bytes 4718600 | tf_op jit(solution)/shard_map/ppermute | solution.py:15
  6.2 0.0 copy-start.2
  6.2 0.0 copy-start.3
  6.2 0.0 copy-start
  6.2 18.0 %fusion.10 = (f32[4096,256]{1,0:T(8,128)}, f32[4096,256]{1,0:T(8,128)}) fusion(s32[256]{0:T(256)S(1)} %iota_add_fusion), kind=kLoop, calls=%fused_computation.17 | loop fusion | flops 15728640 | bytes 8389632 | tf_op jit(solution)/shard_map/cos | solution.py:26
  24.2 0.0 copy-done.2
  24.2 0.0 copy-done.3
  24.2 0.0 copy-done
  24.2 0.0 copy-start.1
  24.3 6.4 %convolution_bitcast_fusion.1.refs_0_.refs_1_ = bf16[12,64,8192]{2,1,0:T(8,128)(2,1)} fusion(bf16[12,16,8192]{2,1,0:T(8,128)(2,1)S(1)} %bitcast.24, s32[64]{0:T(128)S(1)} %get-tuple-element.8), kind=kOutput, calls=%fused_computation.1 | convolution fusion | flops 201327616 | bytes 15728896 | tf_op jit(solution)/shard_map/ps,xsk->xpk/dot_general | solution.py:119
  30.7 0.0 copy-done.1
  30.7 2.6 %fusion.refs_5_.refs_6_ = bf16[8192,256]{1,0:T(8,128)(2,1)S(1)} fusion(f32[4096,256]{1,0:T(8,128)} %get-tuple-element.6, f32[4096,256]{1,0:T(8,128)S(1)} %copy-done.1, f32[256]{0:T(256)S(1)} %add_multiply_fusion), kind=kLoop, calls=%fused_computation.3 | loop fusion | flops 6291456 | bytes 12583936 | tf_op jit(solution)/shard_map/convert_element_type | solution.py:29
  33.3 45.6 %collective-permute-done = bf16[4,8,3,8192]{3,1,2,0:T(8,128)(2,1)} collective-permute-done((bf16[4,8,3,8192]{3,1,2,0:T(8,128)(2,1)}, bf16[4,8,3,8192]{3,1,2,0:T(8,128)(2,1)}, u32[]{:S(2)}, u32[]{:S(2)}) %collective-permute-start) | collective-permute-done | bytes 1572896 | tf_op jit(solution)/shard_map/ppermute | solution.py:15
  78.8 9.6 %convolution_bitcast_fusion.refs_2_.refs_3_ = bf16[12,64,8192]{2,1,0:T(8,128)(2,1)} fusion(bf16[12,8,8192]{2,1,0:T(8,128)(2,1)} %bitcast.7, bf16[12,16,8192]{2,1,0:T(8,128)(2,1)S(1)} %bitcast.25, s32[64]{0:T(128)S(1)} %get-tuple-element.7), kind=kOutput, calls=%fused_computation | convolution fusion | flops 311428608 | bytes 17301760 | tf_op jit(solution)/shard_map/ps,xsk->xpk/dot_general | solution.py:120
  88.4 20.2 %shard_map.46 = f32[8,9,8,256]{3,2,1,0:T(8,128)S(1)} custom-call(bf16[12,64,8192]{2,1,0:T(8,128)(2,1)} %convolution_bitcast_fusion.1.refs_0_.refs_1_, bf16[12,64,8192]{2,1,0:T(8,128)(2,1)} %convolution_bitcast_fusion.1.refs_0_.refs_1_, bf16[12,64,8192]{2,1,0:T(8,128)(2,1)} %convolution_bitcast_fusion.refs_2_.refs_3_, ...), custom_call_target="tpu_custom_call" | custom-call | flops 2491416576 | bytes 34078720 | tf_op jit(solution)/shard_map/pallas_call | solution.py:74
  108.6 24.4 %all_to_all.5 = f32[8,9,8,256]{3,2,1,0:T(8,128)S(1)} all-to-all(f32[8,9,8,256]{3,2,1,0:T(8,128)S(1)} %shard_map.46), channel_id=1, replica_groups=mesh['pair'=64,'win'=8] {'win'}, dimensions={0} | all-to-all | bytes 1179648 | tf_op jit(solution)/shard_map/all_to_all | solution.py:123
  133.0 0.7 reduce_sum.9
  (4 shorter events, 0.1 us)
Async XLA Ops:
  2.7 76.1 %collective-permute-start = (bf16[4,8,3,8192]{3,1,2,0:T(8,128)(2,1)}, bf16[4,8,3,8192]{3,1,2,0:T(8,128)(2,1)}, u32[]{:S(2)}, u32[]{:S(2)}) collective-permute-start(bf16[4,8,3,8192]{3,1,2,0:T(8,128)(2,1)} %slice.3), channel_id=1, source_target_pairs={{8,0},{16,8},{24,16},{32,24},{40,32},{48,40},{56,48},{64,56},{72,6... | collective-permute-start | bytes 4718600 | tf_op jit(solution)/shard_map/ppermute | solution.py:15
  6.2 18.0 %copy-start.2 = (s32[1,64]{1,0:T(1,128)S(1)}, s32[1,64]{1,0:T(1,128)}, u32[]{:S(2)}) copy-start(s32[1,64]{1,0:T(1,128)} %param.6) | copy-start | bytes 772
  6.2 18.0 %copy-start.3 = (s32[1,64]{1,0:T(1,128)S(1)}, s32[1,64]{1,0:T(1,128)}, u32[]{:S(2)}) copy-start(s32[1,64]{1,0:T(1,128)} %param.5) | copy-start | bytes 772
  6.2 18.1 %copy-start = (bf16[4,16,3,8192]{3,1,2,0:T(8,128)(2,1)S(1)}, bf16[4,16,3,8192]{3,1,2,0:T(8,128)(2,1)}, u32[]{:S(2)}) copy-start(bf16[4,16,3,8192]{3,1,2,0:T(8,128)(2,1)} %param.4) | copy-start | bytes 9437188
  24.2 6.4 %copy-start.1 = (f32[4096,256]{1,0:T(8,128)S(1)}, f32[4096,256]{1,0:T(8,128)}, u32[]{:S(2)}) copy-start(f32[4096,256]{1,0:T(8,128)} %get-tuple-element.5) | copy-start | bytes 12582916
